TPU v7x, 256 devices: a whole 4x4x8 slice. The times are simulated.
256 devices in a mesh: rows: 8 (over y_hi, x), vecs: 32 (over y_lo, z, core).
Axes of the slice: x: 4, y: 4 (y_hi: 2, y_lo: 2; y = y_hi * 2 + y_lo), z: 8, core: 2. Of those that a mesh axis runs over, the one named last changes fastest.
Arguments:
- eigvecs: float32 [16384, 4096], P('rows', 'vecs'), may hold values from -6 to 6
- reflectors: float32 [7, 8192, 256], P(None, ('rows', 'vecs')), may hold values from -6 to 6
- offsets: int32 [7, 8], P(None, 'rows'), may hold values from 0 to 1024, as said below
Outputs:
- rotated: float32 [16384, 4096], P('rows', 'vecs')
Inputs may be any that keep to these rules, and one draw needn't show every extreme that they name: `offsets`: in every tick some row block has offset 2048 - 1024 and another has offset 0.
All inputs are finite; a program needn't handle non-finite values.
Results may differ from a plain program's by a relative error of at most 0.00028.
Values sent between devices are 32-bit elements; how exact they have to be, the bound alone decides.
No kernel may reach another device: no remote copies, remote signals or barrier semaphores. Data moves between devices by JAX's collectives and lax.ppermute only.
A program may use at most 128 MiB of HBM per device.

v0:
```python
import jax
import jax.numpy as jnp
from jax import lax
from jax.sharding import PartitionSpec as P

NB = 1024
H = 256
TICKS = 7


def passed_along(x, axis, by):
    size = lax.axis_size(axis)
    return lax.ppermute(x, axis, [(i, (i + by) % size) for i in range(size)])


def matmul_high(left, right):
    return jnp.dot(left, right, precision=lax.Precision.HIGHEST, preferred_element_type=jnp.float32)


def upper_inverse(tri):
    size = tri.shape[0]
    if size <= 32:
        diag_part = jnp.diagonal(tri)
        eye_part = jnp.eye(size, dtype=jnp.float32)
        nilpotent = tri / diag_part[:, None] - eye_part
        product = eye_part - nilpotent
        power = nilpotent
        span = 2
        while span < size:
            power = matmul_high(power, power)
            product = matmul_high(product, eye_part + power)
            span = span * 2
        return product * (1.0 / diag_part)[None, :]
    half = size // 2
    upper_inv = upper_inverse(tri[:half, :half])
    lower_inv = upper_inverse(tri[half:, half:])
    corner = -matmul_high(matmul_high(upper_inv, tri[:half, half:]), lower_inv)
    top = jnp.concatenate([upper_inv, corner], axis=1)
    bottom = jnp.concatenate([jnp.zeros((size - half, half), jnp.float32), lower_inv], axis=1)
    return jnp.concatenate([top, bottom], axis=0)


def apply_block(block, reflector, first_row, gram_matrix):
    window = lax.dynamic_slice_in_dim(block, first_row, NB, 0)
    inverse_t = jnp.triu(gram_matrix, 1) + jnp.diag(jnp.diagonal(gram_matrix)) * 0.5
    project = matmul_high(reflector.T, window)
    weights = matmul_high(upper_inverse(inverse_t), project)
    window = window - matmul_high(reflector, weights)
    return lax.dynamic_update_slice_in_dim(block, window, first_row, 0)


def shards(eigvecs, reflectors, offsets):
    rows_here = eigvecs.shape[0]
    block = eigvecs
    gathered_all = lax.all_gather(reflectors, "vecs", axis=1, tiled=True)
    for step_index in range(TICKS):
        incoming = passed_along(block[rows_here - H :], "rows", 1)
        block = jnp.concatenate([incoming, block[: rows_here - H]], axis=0)
        reflector = gathered_all[step_index]
        gram_matrix = matmul_high(reflector.T, reflector)
        block = apply_block(block, reflector, offsets[step_index, 0], gram_matrix)
    return block


def solution(mesh):
    in_specs = (P("rows", "vecs"), P(None, ("rows", "vecs"), None), P(None, "rows"))
    out_specs = P("rows", "vecs")
    return jax.shard_map(shards, mesh=mesh, in_specs=in_specs, out_specs=out_specs, check_vma=False)
```

profile of v0, /device:TPU:8, one launch (start us, length us, event | category | flops | bytes accessed | tf_op | source)
XLA Modules:
  0.0 484.7 jit_solution(16719153635963538116)
XLA Ops:
  26.4 56.6 %all-gather.2.cloned.1.call-done = f32[7,1024,256]{2,1,0:T(8,128)} async-done(((f32[7,32,256]{2,1,0:T(8,128)}), f32[7,1024,256]{2,1,0:T(8,128)}) %all-gather.2.cloned.1.call-update) | async-done | bytes 7340048 | tf_op jit(solution)/shard_map/all_gather | solution.py:55
  83.0 3.5 fusion.8
  86.5 2.9 gather_fusion
  131.0 3.4 fusion.10
  134.4 2.5 gather_fusion.9
  156.8 3.4 fusion.12
  182.5 3.4 fusion.14
  185.9 2.6 gather_fusion.27
  208.4 3.4 fusion.16
  234.2 3.5 fusion.18
  237.7 2.7 gather_fusion.45
  260.5 3.4 fusion.20
  396.0 2.5 dynamic_update_slice.22
  400.0 7.6 %collective-permute-done.2 = f32[256,128]{0,1:T(8,128)S(1)} collective-permute-done((f32[256,128]{0,1:T(8,128)S(1)}, f32[256,128]{0,1:T(8,128)S(1)}, u32[]{:S(2)}, u32[]{:S(2)}) %collective-permute-start.2) | collective-permute-done | bytes 131104 | tf_op jit(solution)/shard_map/ppermute | solution.py:13
  410.9 2.3 fusion.4
  415.7 8.3 %collective-permute-done.3 = f32[256,128]{0,1:T(8,128)S(1)} collective-permute-done((f32[256,128]{0,1:T(8,128)S(1)}, f32[256,128]{0,1:T(8,128)S(1)}, u32[]{:S(2)}, u32[]{:S(2)}) %collective-permute-start.3) | collective-permute-done | bytes 131104 | tf_op jit(solution)/shard_map/ppermute | solution.py:13
  426.4 2.4 fusion.3
  429.9 8.3 %collective-permute-done.4 = f32[256,128]{0,1:T(8,128)S(1)} collective-permute-done((f32[256,128]{0,1:T(8,128)S(1)}, f32[256,128]{0,1:T(8,128)S(1)}, u32[]{:S(2)}, u32[]{:S(2)}) %collective-permute-start.4) | collective-permute-done | bytes 131104 | tf_op jit(solution)/shard_map/ppermute | solution.py:13
  440.6 2.4 fusion.2
  445.8 8.2 %collective-permute-done.5 = f32[256,128]{0,1:T(8,128)S(1)} collective-permute-done((f32[256,128]{0,1:T(8,128)S(1)}, f32[256,128]{0,1:T(8,128)S(1)}, u32[]{:S(2)}, u32[]{:S(2)}) %collective-permute-start.5) | collective-permute-done | bytes 131104 | tf_op jit(solution)/shard_map/ppermute | solution.py:13
  456.5 2.4 fusion.1
  458.9 2.7 dynamic_update_slice.26
  462.3 8.3 %collective-permute-done.6 = f32[256,128]{0,1:T(8,128)S(1)} collective-permute-done((f32[256,128]{0,1:T(8,128)S(1)}, f32[256,128]{0,1:T(8,128)S(1)}, u32[]{:S(2)}, u32[]{:S(2)}) %collective-permute-start.6) | collective-permute-done | bytes 131104 | tf_op jit(solution)/shard_map/ppermute | solution.py:13
  473.1 2.4 fusion
  (874 shorter events, 304.7 us)
Async XLA Ops:
  6.5 76.5 %all-gather.2.cloned.1.call-start = ((), (), s32[]{:S(2)}) async-start(), calls=%async_computation | async-start | bytes 7569408 | tf_op jit(solution)/shard_map/all_gather | solution.py:55
  8.3 18.0 %collective-permute-start = (f32[256,128]{0,1:T(8,128)S(1)}, f32[256,128]{0,1:T(8,128)S(1)}, u32[]{:S(2)}, u32[]{:S(2)}) collective-permute-start(f32[256,128]{0,1:T(8,128)S(1)} %copy.10), channel_id=1, source_target_pairs={{0,32},{32,64},{64,96},{96,128},{128,160},{160,192},{192,224},{224... | collective-permute-start | bytes 393224 | tf_op jit(solution)/shard_map/ppermute | solution.py:13
  282.8 87.3 %copy-start.48 = (f32[32]{0:T(128)S(1)}, f32[32]{0:T(128)}, u32[]{:S(2)}) copy-start(f32[32]{0:T(128)} %broadcast_divide_fusion.10) | copy-start | bytes 388
  282.8 87.7 %copy-start.38 = (f32[32,32]{1,0:T(8,128)S(1)}, f32[32,32]{1,0:T(8,128)}, u32[]{:S(2)}) copy-start(f32[32,32]{1,0:T(8,128)} %fusion.449) | copy-start | bytes 12292
  282.8 88.2 %copy-start.47 = (f32[32]{0:T(128)S(1)}, f32[32]{0:T(128)}, u32[]{:S(2)}) copy-start(f32[32]{0:T(128)} %broadcast_divide_fusion.11) | copy-start | bytes 388
  283.4 107.7 %collective-permute-start.1 = (f32[256,128]{0,1:T(8,128)}, f32[256,128]{0,1:T(8,128)S(1)}, u32[]{:S(2)}, u32[]{:S(2)}) collective-permute-start(f32[256,128]{0,1:T(8,128)} %slice.842), channel_id=1, source_target_pairs={{0,32},{32,64},{64,96},{96,128},{128,160},{160,192},{192,224},{224... | collective-permute-start | bytes 393224 | tf_op jit(solution)/shard_map/ppermute | solution.py:13
  286.6 85.5 %copy-start.36 = (f32[32,32]{1,0:T(8,128)S(1)}, f32[32,32]{1,0:T(8,128)}, u32[]{:S(2)}) copy-start(f32[32,32]{1,0:T(8,128)} %fusion.446) | copy-start | bytes 12292
  288.0 84.8 %copy-start.37 = (f32[32,32]{1,0:T(8,128)S(1)}, f32[32,32]{1,0:T(8,128)}, u32[]{:S(2)}) copy-start(f32[32,32]{1,0:T(8,128)} %fusion.443) | copy-start | bytes 12292
  289.1 84.1 %copy-start.46 = (f32[32]{0:T(128)S(1)}, f32[32]{0:T(128)}, u32[]{:S(2)}) copy-start(f32[32]{0:T(128)} %broadcast_divide_fusion.13) | copy-start | bytes 388
  290.0 83.6 %copy-start.45 = (f32[32]{0:T(128)S(1)}, f32[32]{0:T(128)}, u32[]{:S(2)}) copy-start(f32[32]{0:T(128)} %broadcast_divide_fusion.12) | copy-start | bytes 388
  291.4 82.8 %copy-start.35 = (f32[32,32]{1,0:T(8,128)S(1)}, f32[32,32]{1,0:T(8,128)}, u32[]{:S(2)}) copy-start(f32[32,32]{1,0:T(8,128)} %fusion.440) | copy-start | bytes 12292
  292.5 82.2 %copy-start.44 = (f32[32]{0:T(128)S(1)}, f32[32]{0:T(128)}, u32[]{:S(2)}) copy-start(f32[32]{0:T(128)} %broadcast_divide_fusion.14) | copy-start | bytes 388
  293.7 81.4 %copy-start.31 = (f32[32,32]{1,0:T(8,128)S(1)}, f32[32,32]{1,0:T(8,128)}, u32[]{:S(2)}) copy-start(f32[32,32]{1,0:T(8,128)} %fusion.437) | copy-start | bytes 12292
  294.8 80.7 %copy-start.42 = (f32[32]{0:T(128)S(1)}, f32[32]{0:T(128)}, u32[]{:S(2)}) copy-start(f32[32]{0:T(128)} %broadcast_divide_fusion.15) | copy-start | bytes 388
  295.3 81.3 %copy-start.33 = (f32[32,32]{1,0:T(8,128)S(1)}, f32[32,32]{1,0:T(8,128)}, u32[]{:S(2)}) copy-start(f32[32,32]{1,0:T(8,128)} %fusion.482) | copy-start | bytes 12292
  296.7 80.6 %copy-start.34 = (f32[32,32]{1,0:T(8,128)S(1)}, f32[32,32]{1,0:T(8,128)}, u32[]{:S(2)}) copy-start(f32[32,32]{1,0:T(8,128)} %fusion.479) | copy-start | bytes 12292
  298.0 80.4 %copy-start.32 = (f32[32,32]{1,0:T(8,128)S(1)}, f32[32,32]{1,0:T(8,128)}, u32[]{:S(2)}) copy-start(f32[32,32]{1,0:T(8,128)} %fusion.476) | copy-start | bytes 12292
  299.8 79.1 %copy-start.43 = (f32[32]{0:T(128)S(1)}, f32[32]{0:T(128)}, u32[]{:S(2)}) copy-start(f32[32]{0:T(128)} %broadcast_divide_fusion.2) | copy-start | bytes 388
  300.0 79.2 %copy-start.30 = (f32[32,32]{1,0:T(8,128)S(1)}, f32[32,32]{1,0:T(8,128)}, u32[]{:S(2)}) copy-start(f32[32,32]{1,0:T(8,128)} %fusion.473) | copy-start | bytes 12292
  398.5 9.0 %collective-permute-start.2 = (f32[256,128]{0,1:T(8,128)S(1)}, f32[256,128]{0,1:T(8,128)S(1)}, u32[]{:S(2)}, u32[]{:S(2)}) collective-permute-start(f32[256,128]{0,1:T(8,128)S(1)} %slice.860), channel_id=1, source_target_pairs={{0,32},{32,64},{64,96},{96,128},{128,160},{160,192},{192,224},{224... | collective-permute-start | bytes 393224 | tf_op jit(solution)/shard_map/ppermute | solution.py:13
  415.0 8.9 %collective-permute-start.3 = (f32[256,128]{0,1:T(8,128)S(1)}, f32[256,128]{0,1:T(8,128)S(1)}, u32[]{:S(2)}, u32[]{:S(2)}) collective-permute-start(f32[256,128]{0,1:T(8,128)S(1)} %slice.878), channel_id=1, source_target_pairs={{0,32},{32,64},{64,96},{96,128},{128,160},{160,192},{192,224},{224... | collective-permute-start | bytes 393224 | tf_op jit(solution)/shard_map/ppermute | solution.py:13
  429.5 8.7 %collective-permute-start.4 = (f32[256,128]{0,1:T(8,128)S(1)}, f32[256,128]{0,1:T(8,128)S(1)}, u32[]{:S(2)}, u32[]{:S(2)}) collective-permute-start(f32[256,128]{0,1:T(8,128)S(1)} %slice.896), channel_id=1, source_target_pairs={{0,32},{32,64},{64,96},{96,128},{128,160},{160,192},{192,224},{224... | collective-permute-start | bytes 393224 | tf_op jit(solution)/shard_map/ppermute | solution.py:13
  445.3 8.7 %collective-permute-start.5 = (f32[256,128]{0,1:T(8,128)S(1)}, f32[256,128]{0,1:T(8,128)S(1)}, u32[]{:S(2)}, u32[]{:S(2)}) collective-permute-start(f32[256,128]{0,1:T(8,128)S(1)} %slice.914), channel_id=1, source_target_pairs={{0,32},{32,64},{64,96},{96,128},{128,160},{160,192},{192,224},{224... | collective-permute-start | bytes 393224 | tf_op jit(solution)/shard_map/ppermute | solution.py:13
  461.6 9.0 %collective-permute-start.6 = (f32[256,128]{0,1:T(8,128)S(1)}, f32[256,128]{0,1:T(8,128)S(1)}, u32[]{:S(2)}, u32[]{:S(2)}) collective-permute-start(f32[256,128]{0,1:T(8,128)S(1)} %slice.932), channel_id=1, source_target_pairs={{0,32},{32,64},{64,96},{96,128},{128,160},{160,192},{192,224},{224... | collective-permute-start | bytes 393224 | tf_op jit(solution)/shard_map/ppermute | solution.py:13
  (33 other events, 1204.6 us)
Sparse Core Ops, SparseCore 0:
  9.2 73.7 all-gather.1
where the time goes:
time: 492 us; the launch traced here: 485 us
  matrix products  242 us (49%)
  waiting for transfers between devices  97.9 us (20%)
  local copies, waits for them, and re-layouts  79.2 us (16%)
  between operations  31.3 us (6%)
  other arithmetic  28.6 us (6%)
  starting transfers between devices  5.72 us (1%)
    dot_general x574, matrix products, matmul_high(): jnp.dot(left, right, precision=lax.Precision.HIGHEST, preferred_element_t...  242 us
    all_gather x1, waiting for transfers between devices, shards(): gathered_all = lax.all_gather(reflectors, 'vecs', axis=1, tiled=True)  56.6 us
    ppermute x7, waiting for transfers between devices, passed_along(): return lax.ppermute(x, axis, [(i, (i + by) % size) for i in range(size)])  40.6 us
    gather x56, local copies, waits for them, and re-layouts, upper_inverse(): diag_part = jnp.diagonal(tri)  40.2 us
    div x56, other arithmetic, upper_inverse(): return product * (1.0 / diag_part)[None, :]  25.5 us
    gather x7, local copies, waits for them, and re-layouts, apply_block(): jnp.diagonal(gram_matrix)  17.7 us
    dynamic_update_slice x8, local copies, waits for them, and re-layouts, apply_block(): return lax.dynamic_update_slice_in_dim(block, window, first_row, 0)  13.6 us
  transfers between devices with their start and end apart: 8, of which 6 were waited for; matrix products, arithmetic and copies ran while one was open for 22% of the time, Pallas kernels for 0%

commit v1 on v0

v1 whole, which is shorter than its diff:
```python
import jax
import jax.numpy as jnp
from jax import lax
from jax.experimental import pallas as pl
from jax.sharding import PartitionSpec as P

NB = 1024
H = 256
TICKS = 7
BASE = 32


def passed_along(x, axis, by):
    size = lax.axis_size(axis)
    return lax.ppermute(x, axis, [(i, (i + by) % size) for i in range(size)])


def matmul_high(left, right):
    return jnp.dot(left, right, precision=lax.Precision.HIGHEST, preferred_element_type=jnp.float32)


def tri_inverse_kernel(g_ref, o_ref):
    g = g_ref[...]
    size = g.shape[0]
    row = lax.broadcasted_iota(jnp.int32, (size, size), 0)
    col = lax.broadcasted_iota(jnp.int32, (size, size), 1)
    eye_mask = row == col
    eye = eye_mask.astype(jnp.float32)
    a = jnp.where(col > row, g, jnp.where(eye_mask, g * 0.5, 0.0))
    diag_col = jnp.sum(jnp.where(eye_mask, a, 0.0), axis=1, keepdims=True)
    diag_row = jnp.sum(jnp.where(eye_mask, a, 0.0), axis=0, keepdims=True)
    same_base = (row // BASE) == (col // BASE)
    nilpotent = jnp.where(same_base, a / diag_col, 0.0) - eye

    def square(_, carry):
        product, power = carry
        power = matmul_high(power, power)
        return matmul_high(product, eye + power), power

    product, _ = lax.fori_loop(0, BASE.bit_length() - 2, square, (eye - nilpotent, nilpotent))
    inv = product * (1.0 / diag_row)
    row_shift = jnp.right_shift(row, BASE.bit_length() - 1)
    col_shift = jnp.right_shift(col, BASE.bit_length() - 1)

    def merge(level, inv):
        row_blk = jnp.right_shift(row_shift, level)
        col_blk = jnp.right_shift(col_shift, level)
        corner_mask = (jnp.bitwise_and(row_blk, 1) == 0) & (col_blk == row_blk + 1)
        upper = jnp.where(corner_mask, a, 0.0)
        return inv - matmul_high(matmul_high(inv, upper), inv)

    inv = lax.fori_loop(0, size.bit_length() - BASE.bit_length(), merge, inv)
    o_ref[...] = inv


def tri_inverse(gram):
    return pl.pallas_call(
        tri_inverse_kernel,
        out_shape=jax.ShapeDtypeStruct(gram.shape, jnp.float32),
    )(gram)


def shards(eigvecs, reflectors, offsets):
    rows_here = eigvecs.shape[0]
    kb = reflectors.shape[-1]
    block = eigvecs
    outgoing = block[rows_here - H :]
    for step_index in range(TICKS):
        reflector = lax.all_gather(reflectors[step_index], "vecs", axis=0, tiled=True)
        gram = lax.dot_general(
            reflector, reflector, (((0,), (0,)), ((), ())),
            precision=lax.Precision.HIGHEST, preferred_element_type=jnp.float32,
        )
        solve = tri_inverse(gram)
        placed = lax.dynamic_update_slice_in_dim(
            jnp.zeros((rows_here, kb), jnp.float32), reflector, offsets[step_index, 0], 0
        )
        own = block[: rows_here - H]
        incoming = passed_along(outgoing, "rows", 1)
        project = lax.dot_general(
            placed[H:], own, (((0,), (0,)), ((), ())),
            precision=lax.Precision.HIGHEST, preferred_element_type=jnp.float32,
        ) + lax.dot_general(
            placed[:H], incoming, (((0,), (0,)), ((), ())),
            precision=lax.Precision.HIGHEST, preferred_element_type=jnp.float32,
        )
        weights = matmul_high(solve, project)
        block = jnp.concatenate([incoming, own], axis=0)
        if step_index + 1 < TICKS:
            outgoing = block[rows_here - H :] - matmul_high(placed[rows_here - H :], weights)
        block = block - matmul_high(placed, weights)
    return block


def solution(mesh):
    in_specs = (P("rows", "vecs"), P(None, ("rows", "vecs"), None), P(None, "rows"))
    out_specs = P("rows", "vecs")
    return jax.shard_map(shards, mesh=mesh, in_specs=in_specs, out_specs=out_specs, check_vma=False)
```

time: 492 us -> 607 us (1.23)
  waiting for transfers between devices: 97.9 us -> 376 us
  matrix products: 242 us -> 74.4 us
  Pallas kernels: 0 us -> 66.4 us
  local copies, waits for them, and re-layouts: 79.2 us -> 46.2 us
  other arithmetic: 28.6 us -> 0.1 us
    all_gather x1 -> x7, waiting for transfers between devices: 56.6 us -> 339 us  [shards(): lax.all_gather(reflectors[step_index], 'vecs', axis=0, tiled=True)]
    dot_general x574 -> x20, matrix products: 242 us -> 21.6 us  [matmul_high(): jnp.dot(left, right, precision=lax.Precision.HIGHEST, preferred_element_t...]
    pallas_call x0 -> x7, Pallas kernels: none -> 66.4 us  [tri_inverse(): pl.pallas_call(tri_inverse_kernel, out_shape=jax.ShapeDtypeStruct(gram.sh...]
    gather x63 -> x0, local copies, waits for them, and re-layouts: 57.9 us -> none  [the longest x56 40.2 us: upper_inverse(): diag_part = jnp.diagonal(tri)]
    dot_general x0 -> x21, matrix products: none -> 52.8 us  [the longest x7 27.2 us: shards(): lax.dot_general(reflector, reflector, (((0,), (0,)), ((), ())), precision...]
    div x56 -> x0, other arithmetic: 25.5 us -> none  [upper_inverse(): return product * (1.0 / diag_part)[None, :]]
    dynamic_update_slice x8 -> x7, local copies, waits for them, and re-layouts: 13.6 us -> 31.1 us  [shards(): lax.dynamic_update_slice_in_dim(jnp.zeros((rows_here, kb), jnp.float32),...]
    another operation x0 -> x7, local copies, waits for them, and re-layouts: none -> 7.71 us
  transfers between devices with their start and end apart: 8 -> 14, of which waited for: 6 -> 12; matrix products, arithmetic and copies ran while one was open for 22% -> 15% of each run, Pallas kernels for 0% -> 11%
where the time goes in v1:
time: 607 us; the launch traced here: 596 us
  waiting for transfers between devices  376 us (62%)
  matrix products  74.4 us (12%)
  Pallas kernels  66.4 us (11%)
  local copies, waits for them, and re-layouts  46.2 us (8%)
  between operations  27.1 us (4%)
    all_gather x7, waiting for transfers between devices, shards(): lax.all_gather(reflectors[step_index], 'vecs', axis=0, tiled=True)  339 us
    pallas_call x7, Pallas kernels, tri_inverse(): pl.pallas_call(tri_inverse_kernel, out_shape=jax.ShapeDtypeStruct(gram.sh...  66.4 us
    ppermute x7, waiting for transfers between devices, passed_along(): return lax.ppermute(x, axis, [(i, (i + by) % size) for i in range(size)])  34.7 us
    dynamic_update_slice x7, local copies, waits for them, and re-layouts, shards(): lax.dynamic_update_slice_in_dim(jnp.zeros((rows_here, kb), jnp.float32),...  31.1 us
    dot_general x7, matrix products, shards(): lax.dot_general(reflector, reflector, (((0,), (0,)), ((), ())), precision...  27.2 us
    dot_general x20, matrix products, matmul_high(): jnp.dot(left, right, precision=lax.Precision.HIGHEST, preferred_element_t...  21.6 us
    dot_general x7, matrix products, shards(): lax.dot_general(placed[H:], own, (((0,), (0,)), ((), ())), precision=lax....  21.4 us
  transfers between devices with their start and end apart: 14, of which 12 were waited for; matrix products, arithmetic and copies ran while one was open for 15% of the time, Pallas kernels for 11%

profile of v1, /device:TPU:8, one launch (start us, length us, event | category | flops | bytes accessed | tf_op | source)
XLA Modules:
  0.0 596.1 jit_solution(11192802771833997696)
XLA Ops:
  30.3 44.7 %all-gather.15.cloned.1.call-done = f32[1,1024,256]{2,1,0:T(8,128)} async-done(((f32[1,32,256]{2,1,0:T(8,128)}), f32[1,1024,256]{2,1,0:T(8,128)}) %all-gather.15.cloned.1.call-update) | async-done | bytes 1048592 | tf_op jit(solution)/shard_map/all_gather | solution.py:69
  75.1 4.9 dynamic_update_slice.21
  85.6 9.4 %shard_map.37 = f32[256,256]{1,0:T(8,128)} custom-call(f32[256,256]{1,0:T(8,128)} %fusion.68.g_ref), custom_call_target="tpu_custom_call" | custom-call | tf_op jit(solution)/shard_map/pallas_call | solution.py:57
  99.4 40.7 %all-gather.17.cloned.1.call-done = f32[1,1024,256]{2,1,0:T(8,128)} async-done(((f32[1,32,256]{2,1,0:T(8,128)}), f32[1,1024,256]{2,1,0:T(8,128)}) %all-gather.17.cloned.1.call-update) | async-done | bytes 1048592 | tf_op jit(solution)/shard_map/all_gather | solution.py:69
  144.3 9.6 %shard_map.38 = f32[256,256]{1,0:T(8,128)} custom-call(f32[256,256]{1,0:T(8,128)} %fusion.66.g_ref), custom_call_target="tpu_custom_call" | custom-call | tf_op jit(solution)/shard_map/pallas_call | solution.py:57
  157.8 47.5 %all-gather.19.cloned.1.call-done = f32[1,1024,256]{2,1,0:T(8,128)} async-done(((f32[1,32,256]{2,1,0:T(8,128)}), f32[1,1024,256]{2,1,0:T(8,128)}) %all-gather.19.cloned.1.call-update) | async-done | bytes 1048592 | tf_op jit(solution)/shard_map/all_gather | solution.py:69
  209.4 9.4 %shard_map.39 = f32[256,256]{1,0:T(8,128)} custom-call(f32[256,256]{1,0:T(8,128)} %fusion.64.g_ref), custom_call_target="tpu_custom_call" | custom-call | tf_op jit(solution)/shard_map/pallas_call | solution.py:57
  218.9 51.5 %all-gather.21.cloned.1.call-done = f32[1,1024,256]{2,1,0:T(8,128)} async-done(((f32[1,32,256]{2,1,0:T(8,128)}), f32[1,1024,256]{2,1,0:T(8,128)}) %all-gather.21.cloned.1.call-update) | async-done | bytes 1048592 | tf_op jit(solution)/shard_map/all_gather | solution.py:69
  274.5 9.6 %shard_map.40 = f32[256,256]{1,0:T(8,128)} custom-call(f32[256,256]{1,0:T(8,128)} %fusion.62.g_ref), custom_call_target="tpu_custom_call" | custom-call | tf_op jit(solution)/shard_map/pallas_call | solution.py:57
  284.1 51.2 %all-gather.23.cloned.1.call-done = f32[1,1024,256]{2,1,0:T(8,128)} async-done(((f32[1,32,256]{2,1,0:T(8,128)}), f32[1,1024,256]{2,1,0:T(8,128)}) %all-gather.23.cloned.1.call-update) | async-done | bytes 1048592 | tf_op jit(solution)/shard_map/all_gather | solution.py:69
  339.5 9.4 %shard_map.41 = f32[256,256]{1,0:T(8,128)} custom-call(f32[256,256]{1,0:T(8,128)} %fusion.60.g_ref), custom_call_target="tpu_custom_call" | custom-call | tf_op jit(solution)/shard_map/pallas_call | solution.py:57
  348.9 51.5 %all-gather.25.cloned.1.call-done = f32[1,1024,256]{2,1,0:T(8,128)} async-done(((f32[1,32,256]{2,1,0:T(8,128)}), f32[1,1024,256]{2,1,0:T(8,128)}) %all-gather.25.cloned.1.call-update) | async-done | bytes 1048592 | tf_op jit(solution)/shard_map/all_gather | solution.py:69
  404.5 9.4 %shard_map.42 = f32[256,256]{1,0:T(8,128)} custom-call(f32[256,256]{1,0:T(8,128)} %fusion.58.g_ref), custom_call_target="tpu_custom_call" | custom-call | tf_op jit(solution)/shard_map/pallas_call | solution.py:57
  413.9 51.6 %all-gather.27.cloned.1.call-done = f32[1,1024,256]{2,1,0:T(8,128)} async-done(((f32[1,32,256]{2,1,0:T(8,128)}), f32[1,1024,256]{2,1,0:T(8,128)}) %all-gather.27.cloned.1.call-update) | async-done | bytes 1048592 | tf_op jit(solution)/shard_map/all_gather | solution.py:69
  469.6 9.4 %shard_map.43 = f32[256,256]{1,0:T(8,128)} custom-call(f32[256,256]{1,0:T(8,128)} %fusion.56.g_ref), custom_call_target="tpu_custom_call" | custom-call | tf_op jit(solution)/shard_map/pallas_call | solution.py:57
  479.2 5.0 dynamic_update_slice.22
  485.6 4.3 dynamic_update_slice.23
  491.5 4.3 dynamic_update_slice.24
  502.4 4.7 dynamic_update_slice.26
  520.2 6.4 %collective-permute-done.2 = f32[256,128]{1,0:T(8,128)S(1)} collective-permute-done((f32[256,128]{1,0:T(8,128)S(1)}, f32[256,128]{1,0:T(8,128)S(1)}, u32[]{:S(2)}, u32[]{:S(2)}) %collective-permute-start.2) | collective-permute-done | bytes 131104 | tf_op jit(solution)/shard_map/ppermute | solution.py:15
  533.3 6.6 %collective-permute-done.3 = f32[256,128]{1,0:T(8,128)S(1)} collective-permute-done((f32[256,128]{1,0:T(8,128)S(1)}, f32[256,128]{1,0:T(8,128)S(1)}, u32[]{:S(2)}, u32[]{:S(2)}) %collective-permute-start.3) | collective-permute-done | bytes 131104 | tf_op jit(solution)/shard_map/ppermute | solution.py:15
  546.6 6.6 %collective-permute-done.4 = f32[256,128]{1,0:T(8,128)S(1)} collective-permute-done((f32[256,128]{1,0:T(8,128)S(1)}, f32[256,128]{1,0:T(8,128)S(1)}, u32[]{:S(2)}, u32[]{:S(2)}) %collective-permute-start.4) | collective-permute-done | bytes 131104 | tf_op jit(solution)/shard_map/ppermute | solution.py:15
  559.9 6.7 %collective-permute-done.5 = f32[256,128]{1,0:T(8,128)S(1)} collective-permute-done((f32[256,128]{1,0:T(8,128)S(1)}, f32[256,128]{1,0:T(8,128)S(1)}, u32[]{:S(2)}, u32[]{:S(2)}) %collective-permute-start.5) | collective-permute-done | bytes 131104 | tf_op jit(solution)/shard_map/ppermute | solution.py:15
  573.4 8.4 %collective-permute-done.6 = f32[256,128]{1,0:T(8,128)S(1)} collective-permute-done((f32[256,128]{1,0:T(8,128)S(1)}, f32[256,128]{1,0:T(8,128)S(1)}, u32[]{:S(2)}, u32[]{:S(2)}) %collective-permute-start.6) | collective-permute-done | bytes 131104 | tf_op jit(solution)/shard_map/ppermute | solution.py:15
  (114 shorter events, 106.0 us)
Async XLA Ops:
  6.5 68.5 %all-gather.15.cloned.1.call-start = ((), (), s32[]{:S(2)}) async-start(), calls=%async_computation | async-start | bytes 1081344 | tf_op jit(solution)/shard_map/all_gather | solution.py:69
  8.1 132.0 %all-gather.17.cloned.1.call-start = ((), (), s32[]{:S(2)}) async-start(), calls=%async_computation.1 | async-start | bytes 1081344 | tf_op jit(solution)/shard_map/all_gather | solution.py:69
  8.9 196.5 %all-gather.19.cloned.1.call-start = ((), (), s32[]{:S(2)}) async-start(), calls=%async_computation.2 | async-start | bytes 1081344 | tf_op jit(solution)/shard_map/all_gather | solution.py:69
  9.6 260.7 %all-gather.21.cloned.1.call-start = ((), (), s32[]{:S(2)}) async-start(), calls=%async_computation.3 | async-start | bytes 1081344 | tf_op jit(solution)/shard_map/all_gather | solution.py:69
  10.2 325.2 %all-gather.23.cloned.1.call-start = ((), (), s32[]{:S(2)}) async-start(), calls=%async_computation.4 | async-start | bytes 1081344 | tf_op jit(solution)/shard_map/all_gather | solution.py:69
  10.8 389.6 %all-gather.25.cloned.1.call-start = ((), (), s32[]{:S(2)}) async-start(), calls=%async_computation.5 | async-start | bytes 1081344 | tf_op jit(solution)/shard_map/all_gather | solution.py:69
  11.4 454.2 %all-gather.27.cloned.1.call-start = ((), (), s32[]{:S(2)}) async-start(), calls=%async_computation.6 | async-start | bytes 1081344 | tf_op jit(solution)/shard_map/all_gather | solution.py:69
  12.3 82.7 %collective-permute-start = (f32[256,128]{1,0:T(8,128)S(1)}, f32[256,128]{1,0:T(8,128)S(1)}, u32[]{:S(2)}, u32[]{:S(2)}) collective-permute-start(f32[256,128]{1,0:T(8,128)S(1)} %slice.150), channel_id=1, source_target_pairs={{0,32},{32,64},{64,96},{96,128},{128,160},{160,192},{192,224},{224... | collective-permute-start | bytes 393224 | tf_op jit(solution)/shard_map/ppermute | solution.py:15
  98.0 414.8 %collective-permute-start.1 = (f32[256,128]{1,0:T(8,128)}, f32[256,128]{1,0:T(8,128)S(1)}, u32[]{:S(2)}, u32[]{:S(2)}) collective-permute-start(f32[256,128]{1,0:T(8,128)} %convolution_subtract_fusion), channel_id=1, source_target_pairs={{0,32},{32,64},{64,96},{96,128},{128,160},{160,192},{192,224},{224... | collective-permute-start | bytes 393224 | tf_op jit(solution)/shard_map/ppermute | solution.py:15
  517.3 9.3 %copy-start = (f32[2048,256]{1,0:T(8,128)S(1)}, f32[2048,256]{1,0:T(8,128)}, u32[]{:S(2)}) copy-start(f32[2048,256]{1,0:T(8,128)} %dynamic_update_slice.23) | copy-start | bytes 6291460
  517.3 9.3 %collective-permute-start.2 = (f32[256,128]{1,0:T(8,128)S(1)}, f32[256,128]{1,0:T(8,128)S(1)}, u32[]{:S(2)}, u32[]{:S(2)}) collective-permute-start(f32[256,128]{1,0:T(8,128)S(1)} %slice_subtract_fusion.5), channel_id=1, source_target_pairs={{0,32},{32,64},{64,96},{96,128},{128,160},{160,192},{192,224},{224... | collective-permute-start | bytes 393224 | tf_op jit(solution)/shard_map/ppermute | solution.py:15
  520.2 10.1 %copy-start.13 = (f32[256,256]{1,0:T(8,128)S(1)}, f32[256,256]{1,0:T(8,128)}, u32[]{:S(2)}) copy-start(f32[256,256]{1,0:T(8,128)} %shard_map.39) | copy-start | bytes 786436
  531.0 8.8 %collective-permute-start.3 = (f32[256,128]{1,0:T(8,128)S(1)}, f32[256,128]{1,0:T(8,128)S(1)}, u32[]{:S(2)}, u32[]{:S(2)}) collective-permute-start(f32[256,128]{1,0:T(8,128)S(1)} %slice_subtract_fusion.3), channel_id=1, source_target_pairs={{0,32},{32,64},{64,96},{96,128},{128,160},{160,192},{192,224},{224... | collective-permute-start | bytes 393224 | tf_op jit(solution)/shard_map/ppermute | solution.py:15
  533.3 10.3 %copy-start.12 = (f32[256,256]{1,0:T(8,128)S(1)}, f32[256,256]{1,0:T(8,128)}, u32[]{:S(2)}) copy-start(f32[256,256]{1,0:T(8,128)} %shard_map.40) | copy-start | bytes 786436
  544.3 8.9 %copy-start.2 = (f32[2048,256]{1,0:T(8,128)S(1)}, f32[2048,256]{1,0:T(8,128)}, u32[]{:S(2)}) copy-start(f32[2048,256]{1,0:T(8,128)} %dynamic_update_slice.25) | copy-start | bytes 6291460
  544.3 8.9 %collective-permute-start.4 = (f32[256,128]{1,0:T(8,128)S(1)}, f32[256,128]{1,0:T(8,128)S(1)}, u32[]{:S(2)}, u32[]{:S(2)}) collective-permute-start(f32[256,128]{1,0:T(8,128)S(1)} %slice_subtract_fusion.4), channel_id=1, source_target_pairs={{0,32},{32,64},{64,96},{96,128},{128,160},{160,192},{192,224},{224... | collective-permute-start | bytes 393224 | tf_op jit(solution)/shard_map/ppermute | solution.py:15
  546.6 10.3 %copy-start.11 = (f32[256,256]{1,0:T(8,128)S(1)}, f32[256,256]{1,0:T(8,128)}, u32[]{:S(2)}) copy-start(f32[256,256]{1,0:T(8,128)} %shard_map.41) | copy-start | bytes 786436
  557.7 8.9 %copy-start.3 = (f32[2048,256]{1,0:T(8,128)S(1)}, f32[2048,256]{1,0:T(8,128)}, u32[]{:S(2)}) copy-start(f32[2048,256]{1,0:T(8,128)} %dynamic_update_slice.26) | copy-start | bytes 6291460
  557.7 8.9 %collective-permute-start.5 = (f32[256,128]{1,0:T(8,128)S(1)}, f32[256,128]{1,0:T(8,128)S(1)}, u32[]{:S(2)}, u32[]{:S(2)}) collective-permute-start(f32[256,128]{1,0:T(8,128)S(1)} %slice_subtract_fusion.1), channel_id=1, source_target_pairs={{0,32},{32,64},{64,96},{96,128},{128,160},{160,192},{192,224},{224... | collective-permute-start | bytes 393224 | tf_op jit(solution)/shard_map/ppermute | solution.py:15
  559.9 10.8 %copy-start.5 = (f32[2048,128]{1,0:T(8,128)}, f32[2048,128]{1,0:T(8,128)S(1)}, u32[]{:S(2)}) copy-start(f32[2048,128]{1,0:T(8,128)S(1)} %maximum_subtract_fusion.4) | copy-start | bytes 3145732
  559.9 10.4 %copy-start.10 = (f32[256,256]{1,0:T(8,128)S(1)}, f32[256,256]{1,0:T(8,128)}, u32[]{:S(2)}) copy-start(f32[256,256]{1,0:T(8,128)} %shard_map.42) | copy-start | bytes 786436
  572.9 9.0 %copy-start.4 = (f32[2048,256]{1,0:T(8,128)S(1)}, f32[2048,256]{1,0:T(8,128)}, u32[]{:S(2)}) copy-start(f32[2048,256]{1,0:T(8,128)} %dynamic_update_slice.27) | copy-start | bytes 6291460
  572.9 9.0 %collective-permute-start.6 = (f32[256,128]{1,0:T(8,128)S(1)}, f32[256,128]{1,0:T(8,128)S(1)}, u32[]{:S(2)}, u32[]{:S(2)}) collective-permute-start(f32[256,128]{1,0:T(8,128)S(1)} %slice_subtract_fusion.2), channel_id=1, source_target_pairs={{0,32},{32,64},{64,96},{96,128},{128,160},{160,192},{192,224},{224... | collective-permute-start | bytes 393224 | tf_op jit(solution)/shard_map/ppermute | solution.py:15
  573.4 12.1 %copy-start.9 = (f32[256,256]{1,0:T(8,128)S(1)}, f32[256,256]{1,0:T(8,128)}, u32[]{:S(2)}) copy-start(f32[256,256]{1,0:T(8,128)} %shard_map.43) | copy-start | bytes 786436
  (6 other events, 27.6 us)
Sparse Core Ops, SparseCore 0:
  9.2 65.7 all-gather.14
  76.8 63.2 all-gather.16
  142.0 63.2 all-gather.18
  207.1 63.2 all-gather.20
  272.1 63.2 all-gather.22
  337.1 63.2 all-gather.24
  402.2 63.2 all-gather.26

commit v2 on v1

v2 whole, which is shorter than its diff:
```python
import jax
import jax.numpy as jnp
from jax import lax
from jax.sharding import PartitionSpec as P

H = 256
TICKS = 7
BASE = 32


def passed_along(x, axis, by):
    size = lax.axis_size(axis)
    return lax.ppermute(x, axis, [(i, (i + by) % size) for i in range(size)])


def matmul_high(left, right):
    return jnp.matmul(left, right, precision=lax.Precision.HIGHEST, preferred_element_type=jnp.float32)


def project_onto(left, right):
    return lax.dot_general(
        left, right, (((left.ndim - 2,), (right.ndim - 2,)), ((), ())),
        precision=lax.Precision.HIGHEST, preferred_element_type=jnp.float32,
    )


def tri_inverses(gram):
    size = gram.shape[-1]
    row = lax.broadcasted_iota(jnp.int32, (size, size), 0)
    col = lax.broadcasted_iota(jnp.int32, (size, size), 1)
    eye_mask = row == col
    eye = eye_mask.astype(jnp.float32)
    a = jnp.where(col > row, gram, jnp.where(eye_mask, gram * 0.5, 0.0))
    diag_part = jnp.sum(jnp.where(eye_mask, a, 0.0), axis=-1)
    same_base = (row // BASE) == (col // BASE)
    nilpotent = jnp.where(same_base, a / diag_part[..., :, None], 0.0) - eye
    product = eye - nilpotent
    power = nilpotent
    span = 2
    while span < BASE:
        power = matmul_high(power, power)
        product = matmul_high(product, eye + power)
        span = span * 2
    inv = product * (1.0 / diag_part)[..., None, :]
    half = BASE
    while half < size:
        corner_mask = ((row // half) % 2 == 0) & ((col // half) == (row // half) + 1)
        upper = jnp.where(corner_mask, a, 0.0)
        inv = inv - matmul_high(matmul_high(inv, upper), inv)
        half = half * 2
    return inv


def placed_reflectors(reflectors, offsets, rows_here):
    nb = reflectors.shape[1]
    index = jnp.arange(rows_here, dtype=jnp.int32)[None, :] - offsets[:, None]
    inside = (index >= 0) & (index < nb)
    taken = jnp.take_along_axis(reflectors, jnp.clip(index, 0, nb - 1)[:, :, None], axis=1)
    return jnp.where(inside[:, :, None], taken, 0.0)


def shards(eigvecs, reflectors, offsets):
    rows_here = eigvecs.shape[0]
    gathered = lax.all_gather(reflectors, "vecs", axis=1, tiled=True)
    gram = jnp.einsum("tkr,tks->trs", gathered, gathered, precision=lax.Precision.HIGHEST, preferred_element_type=jnp.float32)
    solves = tri_inverses(gram)
    placed_all = placed_reflectors(gathered, offsets[:, 0], rows_here)
    block = eigvecs
    outgoing = block[rows_here - H :]
    for step_index in range(TICKS):
        placed = placed_all[step_index]
        own = block[: rows_here - H]
        incoming = passed_along(outgoing, "rows", 1)
        project = project_onto(placed[H:], own) + project_onto(placed[:H], incoming)
        weights = matmul_high(solves[step_index], project)
        block = jnp.concatenate([incoming, own], axis=0)
        if step_index + 1 < TICKS:
            outgoing = block[rows_here - H :] - matmul_high(placed[rows_here - H :], weights)
        block = block - matmul_high(placed, weights)
    return block


def solution(mesh):
    in_specs = (P("rows", "vecs"), P(None, ("rows", "vecs"), None), P(None, "rows"))
    out_specs = P("rows", "vecs")
    return jax.shard_map(shards, mesh=mesh, in_specs=in_specs, out_specs=out_specs, check_vma=False)
```

time: 607 us -> 721 us (1.19)
  local copies, waits for them, and re-layouts: 46.2 us -> 461 us
  waiting for transfers between devices: 376 us -> 115 us
  Pallas kernels: 66.4 us -> 0 us
  matrix products: 74.4 us -> 106 us
  between operations: 27.1 us -> 14.5 us
  other arithmetic: 0.1 us -> 7.52 us
    gather x0 -> x2, local copies, waits for them, and re-layouts: none -> 451 us  [placed_reflectors(): jnp.take_along_axis(reflectors, jnp.clip(index, 0, nb - 1)[:, :, None], a...]
    all_gather x7 -> x1, waiting for transfers between devices: 339 us -> 72.3 us  [shards(): gathered = lax.all_gather(reflectors, 'vecs', axis=1, tiled=True)]
    pallas_call x7 -> x0, Pallas kernels: 66.4 us -> none  [tri_inverse(): pl.pallas_call(tri_inverse_kernel, out_shape=jax.ShapeDtypeStruct(gram.sh...]
    dot_general x41 -> x49, matrix products: 74.4 us -> 106 us  [the longest x34 63 us: matmul_high(): jnp.matmul(left, right, precision=lax.Precision.HIGHEST, preferred_elemen...]
    dynamic_update_slice x7 -> x0, local copies, waits for them, and re-layouts: 31.1 us -> none  [shards(): lax.dynamic_update_slice_in_dim(jnp.zeros((rows_here, kb), jnp.float32),...]
    dot_general x0 -> x3, local copies, waits for them, and re-layouts: none -> 8.54 us  [matmul_high(): jnp.matmul(left, right, precision=lax.Precision.HIGHEST, preferred_elemen...]
    another operation x7 -> x0, local copies, waits for them, and re-layouts: 7.71 us -> none
    ppermute x7, waiting for transfers between devices: 34.7 us -> 42 us  [passed_along(): return lax.ppermute(x, axis, [(i, (i + by) % size) for i in range(size)])]
  transfers between devices with their start and end apart: 14 -> 8, of which waited for: 12 -> 7; matrix products, arithmetic and copies ran while one was open for 15% -> 77% of each run, Pallas kernels for 11% -> 0%
where the time goes in v2:
time: 721 us; the launch traced here: 708 us
  local copies, waits for them, and re-layouts  461 us (64%)
  waiting for transfers between devices  115 us (16%)
  matrix products  106 us (15%)
  between operations  14.5 us (2%)
  other arithmetic  7.52 us (1%)
    gather x2, local copies, waits for them, and re-layouts, placed_reflectors(): jnp.take_along_axis(reflectors, jnp.clip(index, 0, nb - 1)[:, :, None], a...  451 us
    all_gather x1, waiting for transfers between devices, shards(): gathered = lax.all_gather(reflectors, 'vecs', axis=1, tiled=True)  72.3 us
    dot_general x34, matrix products, matmul_high(): jnp.matmul(left, right, precision=lax.Precision.HIGHEST, preferred_elemen...  63 us
    ppermute x7, waiting for transfers between devices, passed_along(): return lax.ppermute(x, axis, [(i, (i + by) % size) for i in range(size)])  42 us
    dot_general x14, matrix products, project_onto(): lax.dot_general(left, right, (((left.ndim - 2,), (right.ndim - 2,)), ((),...  25.7 us
    dot_general x1, matrix products, shards(): jnp.einsum('tkr,tks->trs', gathered, gathered, precision=lax.Precision.HI...  17.4 us
  transfers between devices with their start and end apart: 8, of which 7 were waited for; matrix products, arithmetic and copies ran while one was open for 77% of the time, Pallas kernels for 0%

profile of v2, /device:TPU:8, one launch (start us, length us, event | category | flops | bytes accessed | tf_op | source)
XLA Modules:
  0.0 708.2 jit_solution(12353727919039073389)
XLA Ops:
  10.7 72.3 %all-gather.2.cloned.1.call-done = f32[7,1024,256]{2,1,0:T(8,128)} async-done(((f32[7,32,256]{2,1,0:T(8,128)}), f32[7,1024,256]{2,1,0:T(8,128)}) %all-gather.2.cloned.1.call-update) | async-done | bytes 7340048 | tf_op jit(solution)/shard_map/all_gather | solution.py:64
  83.0 17.4 %select_reduce_fusion = (f32[7,256]{1,0:T(8,128)S(1)}, f32[7,256,256]{1,2,0:T(8,128)S(1)}) fusion(pred[256,256]{0,1:T(8,128)(4,1)S(1)} %get-tuple-element.12, pred[256,256]{0,1:T(8,128)(4,1)S(1)} %get-tuple-element.11, f32[7,1024,256]{2,1,0:T(8,128)} %all-gather.2.cloned.1.call-done), kind=kOutput, calls=%fused_computation.46 | convolution fusion | flops 5639436288 | bytes 9313280 | tf_op jit(solution)/shard_map/tkr,tks->trs/dot_general | solution.py:65
  100.4 5.5 fusion.49
  105.9 3.1 copy.12
  109.0 5.1 fusion.101
  116.9 5.2 fusion.102
  124.8 5.3 fusion.103
  130.1 3.8 fusion.26
  153.2 451.4 %gather_fusion = f32[14336,256]{1,0:T(8,128)} fusion(f32[7,1024,256]{2,1,0:T(8,128)} %all-gather.2.cloned.1.call-done, s32[14336]{0:T(1024)S(1)} %reshape.126), kind=kCustom, calls=%fused_computation | custom fusion | bytes 29474816 | tf_op jit(solution)/shard_map/jit(take_along_axis)/gather | solution.py:58
  604.6 6.6 select_select_fusion
  611.2 3.1 fusion.13
  618.2 7.0 collective-permute-done.1
  625.8 3.1 fusion.31
  632.2 6.6 collective-permute-done.2
  639.4 3.1 fusion.32
  645.4 6.6 collective-permute-done.3
  652.6 3.1 fusion.33
  658.7 6.6 collective-permute-done.4
  666.0 3.1 fusion.34
  672.0 6.7 collective-permute-done.5
  679.3 3.1 fusion.35
  685.5 8.5 %collective-permute-done.6 = f32[256,128]{1,0:T(8,128)S(1)} collective-permute-done((f32[256,128]{1,0:T(8,128)S(1)}, f32[256,128]{1,0:T(8,128)S(1)}, u32[]{:S(2)}, u32[]{:S(2)}) %collective-permute-start.6) | collective-permute-done | bytes 131104 | tf_op jit(solution)/shard_map/ppermute | solution.py:13
  694.6 3.1 fusion.36
  698.1 2.8 maximum_subtract_fusion.5
  (84 shorter events, 51.8 us)
Async XLA Ops:
  6.5 3.2 copy-start.5
  6.5 76.4 %all-gather.2.cloned.1.call-start = ((), (), s32[]{:S(2)}) async-start(), calls=%async_computation | async-start | bytes 7569408 | tf_op jit(solution)/shard_map/all_gather | solution.py:64
  8.2 606.1 %collective-permute-start = (f32[256,128]{1,0:T(8,128)S(1)}, f32[256,128]{1,0:T(8,128)S(1)}, u32[]{:S(2)}, u32[]{:S(2)}) collective-permute-start(f32[256,128]{1,0:T(8,128)S(1)} %slice.230), channel_id=1, source_target_pairs={{0,32},{32,64},{64,96},{96,128},{128,160},{160,192},{192,224},{224... | collective-permute-start | bytes 393224 | tf_op jit(solution)/shard_map/ppermute | solution.py:13
  124.8 5.3 copy-start.4
  130.1 3.9 copy-start.1
  133.9 2.0 copy-start.2
  604.6 6.6 copy-start.3
  611.2 5.1 slice-start.1
  615.6 9.6 %collective-permute-start.1 = (f32[256,128]{1,0:T(8,128)S(1)}, f32[256,128]{1,0:T(8,128)S(1)}, u32[]{:S(2)}, u32[]{:S(2)}) collective-permute-start(f32[256,128]{1,0:T(8,128)S(1)} %convolution_subtract_fusion.3), channel_id=1, source_target_pairs={{0,32},{32,64},{64,96},{96,128},{128,160},{160,192},{192,224},{224... | collective-permute-start | bytes 393224 | tf_op jit(solution)/shard_map/ppermute | solution.py:13
  629.7 9.1 %collective-permute-start.2 = (f32[256,128]{1,0:T(8,128)S(1)}, f32[256,128]{1,0:T(8,128)S(1)}, u32[]{:S(2)}, u32[]{:S(2)}) collective-permute-start(f32[256,128]{1,0:T(8,128)S(1)} %slice_subtract_fusion.5), channel_id=1, source_target_pairs={{0,32},{32,64},{64,96},{96,128},{128,160},{160,192},{192,224},{224... | collective-permute-start | bytes 393224 | tf_op jit(solution)/shard_map/ppermute | solution.py:13
  643.2 8.8 %collective-permute-start.3 = (f32[256,128]{1,0:T(8,128)S(1)}, f32[256,128]{1,0:T(8,128)S(1)}, u32[]{:S(2)}, u32[]{:S(2)}) collective-permute-start(f32[256,128]{1,0:T(8,128)S(1)} %slice_subtract_fusion.3), channel_id=1, source_target_pairs={{0,32},{32,64},{64,96},{96,128},{128,160},{160,192},{192,224},{224... | collective-permute-start | bytes 393224 | tf_op jit(solution)/shard_map/ppermute | solution.py:13
  656.5 8.9 %collective-permute-start.4 = (f32[256,128]{1,0:T(8,128)S(1)}, f32[256,128]{1,0:T(8,128)S(1)}, u32[]{:S(2)}, u32[]{:S(2)}) collective-permute-start(f32[256,128]{1,0:T(8,128)S(1)} %slice_subtract_fusion.4), channel_id=1, source_target_pairs={{0,32},{32,64},{64,96},{96,128},{128,160},{160,192},{192,224},{224... | collective-permute-start | bytes 393224 | tf_op jit(solution)/shard_map/ppermute | solution.py:13
  669.8 8.9 %collective-permute-start.5 = (f32[256,128]{1,0:T(8,128)S(1)}, f32[256,128]{1,0:T(8,128)S(1)}, u32[]{:S(2)}, u32[]{:S(2)}) collective-permute-start(f32[256,128]{1,0:T(8,128)S(1)} %slice_subtract_fusion.1), channel_id=1, source_target_pairs={{0,32},{32,64},{64,96},{96,128},{128,160},{160,192},{192,224},{224... | collective-permute-start | bytes 393224 | tf_op jit(solution)/shard_map/ppermute | solution.py:13
  672.0 10.8 %copy-start = (f32[2048,128]{1,0:T(8,128)}, f32[2048,128]{1,0:T(8,128)S(1)}, u32[]{:S(2)}) copy-start(f32[2048,128]{1,0:T(8,128)S(1)} %maximum_subtract_fusion.4) | copy-start | bytes 3145732
  683.2 2.3 slice-start
  685.0 9.0 %collective-permute-start.6 = (f32[256,128]{1,0:T(8,128)S(1)}, f32[256,128]{1,0:T(8,128)S(1)}, u32[]{:S(2)}, u32[]{:S(2)}) collective-permute-start(f32[256,128]{1,0:T(8,128)S(1)} %slice_subtract_fusion.2), channel_id=1, source_target_pairs={{0,32},{32,64},{64,96},{96,128},{128,160},{160,192},{192,224},{224... | collective-permute-start | bytes 393224 | tf_op jit(solution)/shard_map/ppermute | solution.py:13
Sparse Core Ops, SparseCore 0:
  9.2 73.7 all-gather.1
